TPU v7x, 256 devices: a whole 4x4x8 slice. The times are simulated.
256 devices in a mesh: dp: 32 (over z, x_lo, core), factor: 8 (over y, x_hi).
Axes of the slice: x: 4 (x_hi: 2, x_lo: 2; x = x_hi * 2 + x_lo), y: 4, z: 8, core: 2. Of those that a mesh axis runs over, the one named last changes fastest.
Arguments:
- activations: bfloat16 [65536, 14336], P('dp', 'factor'), may hold values from -6 to 6
- out_grads: bfloat16 [65536, 4096], P('dp', 'factor'), may hold values from -6 to 6
- proj_in: bfloat16 [14336, 256], P('factor'), may hold values from -0.046875 to 0.046875
- proj_out: bfloat16 [4096, 256], P('factor'), may hold values from -0.09375 to 0.09375
- basis_in: bfloat16 [256, 256], replicated, may hold values from -0.375 to 0.375
- basis_out: bfloat16 [256, 256], replicated, may hold values from -0.375 to 0.375
- eigen_values: float32 [256, 256], P('factor'), may hold values from 0.01 to 10
- query_in: bfloat16 [256, 8, 256], P('dp'), may hold values from -3 to 3
- query_out: bfloat16 [256, 8, 256], P('dp'), may hold values from -3 to 3
- lengths: int32 [32, 16], P('dp'), may hold values from 1 to 256, 2048 in all within a row
- continues: int32 [32], replicated, may hold values from 0 to 1, as said below
- owners: int32 [512, 1], replicated, may hold values from 0 to 31; in each aligned block of 512 rows (0 to 511, 512 to 1023, ...) at most 32 rows name the same one
Outputs:
- influence: float32 [1024, 256], P('dp')
Inputs may be any that keep to these rules, and one draw needn't show every extreme that they name: `lengths`: each row sums to 2048. `continues`: the flags of sequences 0, 15, 16 and 30 are 1; the flag of the last sequence is not read. `owners`: no dp index owns more than 32 document numbers, and one owns exactly 32.
All inputs are finite; a program needn't handle non-finite values.
Results may differ from a plain program's by a relative error of at most 0.0027.
Values may be sent and summed in bfloat16 or wider, within the bound.
No kernel may reach another device: no remote copies, remote signals or barrier semaphores. Data moves between devices by JAX's collectives and lax.ppermute only.
A program may use at most 64 MiB of HBM per device.

v0:
```python
import jax
import jax.numpy as jnp
from jax import lax
from jax.sharding import PartitionSpec as P

OWN_CAP = 32
DAMPING = 0.1
EPSILON = 1e-06


def from_behind(block, axis, distance):
    devices = range(lax.axis_size(axis))
    route = [(i - distance, i) for i in devices if i - distance in devices]
    return lax.ppermute(block, axis, route)


def per_device(
    activations,
    out_grads,
    proj_in,
    proj_out,
    basis_in,
    basis_out,
    eigen_values,
    query_in,
    query_out,
    lengths,
    continues,
    owners,
):
    tokens_here = activations.shape[0]
    pieces = lengths.shape[1]
    rank_slice = eigen_values.shape[0]
    rank_in = basis_in.shape[0]
    factor_index = lax.axis_index("factor")
    data_index = lax.axis_index("dp")
    data_count = lax.axis_size("dp")
    highest = lax.Precision.HIGHEST
    in_part = jnp.dot(activations, proj_in, preferred_element_type=jnp.float32)
    out_part = jnp.dot(out_grads, proj_out, preferred_element_type=jnp.float32)
    basis_in_wide = basis_in.astype(jnp.float32)
    basis_out_wide = basis_out.astype(jnp.float32)
    rot_in = lax.psum(jnp.dot(in_part, basis_in_wide, precision=highest), "factor")
    rot_out_rows = lax.psum_scatter(
        lax.dot_general(basis_out_wide, out_part, (((0,), (1,)), ((), ())), precision=highest),
        "factor",
        scatter_dimension=0,
        tiled=True,
    )
    piece_lengths = lengths[0]
    piece_ends = jnp.cumsum(piece_lengths)
    piece_starts = piece_ends - piece_lengths
    position = jnp.arange(tokens_here, dtype=jnp.int32)[:, None]
    member = ((position >= piece_starts[None, :]) & (position < piece_ends[None, :])).astype(
        jnp.float32
    )
    stacked = (member[:, :, None] * rot_out_rows.T[:, None, :]).reshape(
        tokens_here, pieces * rank_slice
    )
    grad_rows = lax.dot_general(stacked, rot_in, (((0,), (0,)), ((), ())), precision=highest)
    grad_rows = grad_rows.reshape(pieces, rank_slice * rank_in)
    preceding = from_behind(grad_rows[pieces - 1].astype(jnp.bfloat16), "dp", 1).astype(jnp.float32)
    joined_next = jnp.where(data_index < data_count - 1, continues[data_index], 0).astype(
        jnp.float32
    )
    joined_prev = jnp.where(data_index > 0, continues[jnp.maximum(data_index - 1, 0)], 0).astype(
        jnp.float32
    )
    grad_rows = grad_rows.at[0].add(joined_prev * preceding)
    grad_rows = grad_rows.at[pieces - 1].multiply(1.0 - joined_next)
    scale = (1.0 / (eigen_values + DAMPING)).reshape(-1)
    self_part = jnp.sum(grad_rows * grad_rows * scale[None, :], axis=1)
    grad_low = grad_rows.astype(jnp.bfloat16)
    basis_cut = lax.dynamic_slice_in_dim(basis_out_wide, factor_index * rank_slice, rank_slice, 1)
    q_out = jnp.einsum("qtk,kl->qtl", query_out.astype(jnp.float32), basis_cut, precision=highest)
    q_in = jnp.einsum("qtk,kl->qtl", query_in.astype(jnp.float32), basis_in_wide, precision=highest)
    outer = jnp.einsum("qti,qtj->qij", q_out, q_in, precision=highest)
    part = lax.dot_general(
        grad_low,
        lax.all_gather(
            (outer.reshape(query_in.shape[0], rank_slice * rank_in) * scale[None, :]).astype(
                jnp.bfloat16
            ),
            "dp",
            axis=0,
            tiled=True,
        ),
        (((1,), (1,)), ((), ())),
        preferred_element_type=jnp.float32,
    )
    own_all = owners[:, 0]
    doc_count = own_all.shape[0]
    mine_ids = data_index * pieces + jnp.arange(pieces, dtype=jnp.int32)
    own_mine = lax.dynamic_slice_in_dim(own_all, data_index * pieces, pieces)
    earlier = (own_all[None, :] == own_mine[:, None]) & (
        jnp.arange(doc_count, dtype=jnp.int32)[None, :] < mine_ids[:, None]
    )
    rank_mine = jnp.sum(earlier.astype(jnp.int32), axis=1)
    slot_index = own_mine * OWN_CAP + rank_mine
    slot_rows = data_count * OWN_CAP
    placing = (jnp.arange(slot_rows, dtype=jnp.int32)[:, None] == slot_index[None, :]).astype(
        jnp.float32
    )
    raw_total, self_total = lax.psum((part, self_part), "factor")
    relative = raw_total / jnp.sqrt(self_total + EPSILON)[:, None]
    placed = jnp.dot(placing, relative, precision=highest)
    return lax.psum_scatter(placed, "dp", scatter_dimension=0, tiled=True)


def solution(mesh):
    placed = (
        P("dp", "factor"),
        P("dp", "factor"),
        P("factor", None),
        P("factor", None),
        P(),
        P(),
        P("factor", None),
        P("dp", None, None),
        P("dp", None, None),
        P("dp", None),
        P(),
        P(),
    )
    return jax.shard_map(
        per_device, mesh=mesh, in_specs=placed, out_specs=P("dp", None), check_vma=False
    )
```

profile of v0, /device:TPU:8, one launch (start us, length us, event | category | flops | bytes accessed | tf_op | source)
XLA Modules:
  0.0 394.8 jit_solution(14859609049050436812)
XLA Ops:
  7.4 1.6 copy-done
  9.0 1.7 fusion.17
  10.6 2.4 convolution_bitcast_fusion
  13.1 2.9 copy.22
  16.1 1.1 copy-done.8
  17.2 5.3 %fusion.18 = f32[2048,256]{1,0:T(8,128)S(1)} fusion(bf16[2048,1792]{1,0:T(8,128)(2,1)} %param.16, bf16[1792,256]{1,0:T(8,128)(2,1)S(1)} %copy-done.8), kind=kOutput, calls=%fused_computation.39 | convolution fusion | flops 1879048192 | bytes 10354688 | tf_op jit(solution)/shard_map/dot_general | solution.py:39
  22.5 2.4 fusion.19
  25.0 0.6 copy-done.4
  25.8 0.2 convolution_bitcast_fusion.2
  26.0 0.5 convolution_bitcast_fusion.1
  26.7 0.7 multiply_convert_fusion
  27.5 0.7 fusion.16
  29.8 0.2 convert_reduce_fusion
  30.1 70.0 %reduce-scatter.7.cloned.1.call-done = f32[32,2048]{1,0:T(8,128)} async-done(((f32[256,2048]{1,0:T(8,128)}), f32[32,2048]{1,0:T(8,128)}) %reduce-scatter.7.cloned.1.call-update) | async-done | bytes 262160
  100.2 3.4 broadcast_multiply_fusion
  103.6 108.7 %all-reduce.3.cloned.1.call-done = f32[2048,256]{1,0:T(8,128)} async-done(((f32[2048,256]{1,0:T(8,128)}), f32[2048,256]{1,0:T(8,128)}) %all-reduce.3.cloned.1.call-update) | async-done | bytes 2097168 | tf_op jit(solution)/shard_map/psum | solution.py:43
  212.3 6.0 %fusion.20 = f32[512,256]{1,0:T(8,128)S(1)} fusion(f32[2048,512]{0,1:T(8,128)} %bitcast.57, f32[2048,256]{1,0:T(8,128)} %all-reduce.3.cloned.1.call-done), kind=kOutput, calls=%fused_computation.41 | convolution fusion | flops 3221225472 | bytes 6815744 | tf_op jit(solution)/shard_map/dot_general | solution.py:60
  218.3 1.6 collective-permute-start
  220.1 0.7 collective-permute-done
  221.1 0.2 multiply_reduce_fusion
  221.3 3.4 fusion.1
  224.7 38.6 %all-reduce = (f32[16,256]{1,0:T(8,128)S(1)}, f32[16]{0:T(128)S(1)}) all-reduce(f32[16,256]{1,0:T(8,128)S(1)} %fusion.1, f32[16]{0:T(128)S(1)} %multiply_reduce_fusion), channel_id=1, replica_groups=mesh['dp'=32,'factor'=8] {'factor'}, use_global_device_ids=true, to_apply=%region_4.5 | all-reduce | flops 4112 | bytes 32896 | tf_op jit(solution)/shard_map/psum | solution.py:104
  263.3 1.6 fusion
  264.9 122.4 %reduce-scatter.5.cloned.1.call-done = f32[32,256]{1,0:T(8,128)} async-done(((f32[1024,256]{1,0:T(8,128)}), f32[32,256]{1,0:T(8,128)}) %reduce-scatter.5.cloned.1.call-update) | async-done | bytes 32784 | tf_op jit(solution)/shard_map/reduce_scatter | solution.py:107
  (48 shorter events, 1.6 us)
Async XLA Ops:
  7.4 1.6 copy-start
  7.4 3.3 copy-start.2
  7.4 92.8 %reduce-scatter.7.cloned.1.call-start = ((), (), s32[]{:S(2)}) async-start(), calls=%async_computation.5 | async-start | bytes 2359296
  16.0 1.2 copy-start.8
  16.0 6.5 %copy-start.1 = (bf16[256,256]{1,0:T(8,128)(2,1)S(1)}, bf16[256,256]{1,0:T(8,128)(2,1)}, u32[]{:S(2)}) copy-start(bf16[256,256]{1,0:T(8,128)(2,1)} %param.20) | copy-start | bytes 393220
  16.0 196.3 %all-reduce.3.cloned.1.call-start = ((), (), s32[]{:S(2)}) async-start(), calls=%async_computation.2 | async-start | bytes 4194304 | tf_op jit(solution)/shard_map/psum | solution.py:43
  24.9 0.8 copy-start.4
  24.9 0.8 copy-start.3
  24.9 1.0 copy-start.9
  24.9 2.6 copy-start.6
  24.9 3.9 copy-start.7
  24.9 4.8 %copy-start.5 = (s32[512,1]{0,1:T(1,128)S(1)}, s32[512,1]{0,1:T(1,128)}, u32[]{:S(2)}) copy-start(s32[512,1]{0,1:T(1,128)} %param.27) | copy-start | bytes 6148
  24.9 196.4 %all-gather.2.cloned.1.call-start = ((), (), s32[]{:S(2)}) async-start(), calls=%async_computation.3 | async-start | bytes 4325376 | tf_op jit(solution)/shard_map/all_gather | solution.py:80
  27.4 359.9 %reduce-scatter.5.cloned.1.call-start = ((), (), s32[]{:S(2)}) async-start(), calls=%async_computation.4 | async-start | bytes 1081344 | tf_op jit(solution)/shard_map/reduce_scatter | solution.py:107
  218.3 2.4 collective-permute-start
Sparse Core Ops, SparseCore 0:
  16.1 83.9 reduce-scatter.6
  102.8 109.3 all-reduce.2
Sparse Core Ops, SparseCore 1:
  27.5 70.0 all-gather.1
  265.0 122.3 reduce-scatter.4
where the time goes:
time: 395 us
  waiting for transfers between devices  302 us (76%)
  blocking collectives  38.6 us (10%)
  matrix products  23.6 us (6%)
  between operations  16.4 us (4%)
  local copies, waits for them, and re-layouts  7.7 us (2%)
  other arithmetic  4.88 us (1%)
    reduce_scatter x1, waiting for transfers between devices, per_device(): return lax.psum_scatter(placed, 'dp', scatter_dimension=0, tiled=True)  122 us
    psum x1, waiting for transfers between devices, per_device(): lax.psum(jnp.dot(in_part, basis_in_wide, precision=highest), 'factor')  109 us
    unnamed x5, waiting for transfers between devices  70.1 us
    psum x1, blocking collectives, per_device(): raw_total, self_total = lax.psum((part, self_part), 'factor')  38.6 us
  transfers between devices with their start and end apart: 5, of which 4 were waited for; matrix products, arithmetic and copies ran while one was open for 5% of the time, Pallas kernels for 0%

commit v1 on v0

--- a/solution.py
+++ b/solution.py
@@ -40,7 +40,8 @@
     out_part = jnp.dot(out_grads, proj_out, preferred_element_type=jnp.float32)
     basis_in_wide = basis_in.astype(jnp.float32)
     basis_out_wide = basis_out.astype(jnp.float32)
-    rot_in = lax.psum(jnp.dot(in_part, basis_in_wide, precision=highest), "factor")
+    shard_in = jnp.dot(in_part, basis_in_wide, precision=highest)
+    rot_in = lax.all_gather(shard_in, "factor").sum(axis=0)
     rot_out_rows = lax.psum_scatter(
         lax.dot_general(basis_out_wide, out_part, (((0,), (1,)), ((), ())), precision=highest),
         "factor",

time: 395 us -> 522 us (1.32)
  waiting for transfers between devices: 302 us -> 421 us
  other arithmetic: 4.88 us -> 13.4 us
    all_gather x0 -> x1, waiting for transfers between devices: none -> 185 us  [per_device(): rot_in = lax.all_gather(shard_in, 'factor').sum(axis=0)]
    psum x1 -> x0, waiting for transfers between devices: 109 us -> none  [per_device(): lax.psum(jnp.dot(in_part, basis_in_wide, precision=highest), 'factor')]
    all_gather x1, waiting for transfers between devices: 0.02 us -> 50.2 us  [per_device(): lax.all_gather((outer.reshape(query_in.shape[0], rank_slice * rank_in) *...]
    reduce_sum x0 -> x1, other arithmetic: none -> 8.51 us  [per_device(): rot_in = lax.all_gather(shard_in, 'factor').sum(axis=0)]
    reduce_scatter x1, waiting for transfers between devices: 122 us -> 116 us  [per_device(): return lax.psum_scatter(placed, 'dp', scatter_dimension=0, tiled=True)]
  transfers between devices with their start and end apart: 5 -> 5, of which waited for: 4 -> 5; matrix products, arithmetic and copies ran while one was open for 5% -> 6% of each run, Pallas kernels for 0% -> 0%
where the time goes in v1:
time: 522 us
  waiting for transfers between devices  421 us (81%)
  blocking collectives  39.5 us (8%)
  matrix products  23.6 us (5%)
  between operations  14.7 us (3%)
  other arithmetic  13.4 us (3%)
  local copies, waits for them, and re-layouts  7.66 us (1%)
    all_gather x1, waiting for transfers between devices, per_device(): rot_in = lax.all_gather(shard_in, 'factor').sum(axis=0)  185 us
    reduce_scatter x1, waiting for transfers between devices, per_device(): return lax.psum_scatter(placed, 'dp', scatter_dimension=0, tiled=True)  116 us
    unnamed x5, waiting for transfers between devices  69.7 us
    all_gather x1, waiting for transfers between devices, per_device(): lax.all_gather((outer.reshape(query_in.shape[0], rank_slice * rank_in) *...  50.2 us
    psum x1, blocking collectives, per_device(): raw_total, self_total = lax.psum((part, self_part), 'factor')  39.5 us
  transfers between devices with their start and end apart: 5, of which 5 were waited for; matrix products, arithmetic and copies ran while one was open for 6% of the time, Pallas kernels for 0%

profile of v1, /device:TPU:8, one launch (start us, length us, event | category | flops | bytes accessed | tf_op | source)
XLA Modules:
  0.0 521.6 jit_solution(9944237145468364478)
XLA Ops:
  6.5 1.6 copy-done
  8.1 1.7 fusion.17
  9.8 2.4 convolution_bitcast_fusion
  12.2 2.9 copy.22
  15.2 1.1 copy-done.8
  16.3 5.3 %fusion.18 = f32[2048,256]{1,0:T(8,128)S(1)} fusion(bf16[2048,1792]{1,0:T(8,128)(2,1)} %param.16, bf16[1792,256]{1,0:T(8,128)(2,1)S(1)} %copy-done.8), kind=kOutput, calls=%fused_computation.39 | convolution fusion | flops 1879048192 | bytes 10354688 | tf_op jit(solution)/shard_map/dot_general | solution.py:39
  21.6 2.5 fusion.19
  24.2 0.6 copy-done.4
  24.9 0.2 convolution_bitcast_fusion.2
  25.3 0.5 convolution_bitcast_fusion.1
  25.9 0.7 multiply_convert_fusion
  26.7 0.6 fusion.16
  29.3 69.7 %reduce-scatter.7.cloned.1.call-done = f32[32,2048]{1,0:T(8,128)} async-done(((f32[256,2048]{1,0:T(8,128)}), f32[32,2048]{1,0:T(8,128)}) %reduce-scatter.7.cloned.1.call-update) | async-done | bytes 262160
  99.0 3.4 broadcast_multiply_fusion
  102.4 184.6 %all-gather.6.cloned.1.call-done = f32[16384,256]{1,0:T(8,128)} async-done(((f32[2048,256]{1,0:T(8,128)}), f32[16384,256]{1,0:T(8,128)}) %all-gather.6.cloned.1.call-update) | async-done | bytes 16777232 | tf_op jit(solution)/shard_map/all_gather | solution.py:44
  287.0 8.5 %reduce_sum.28 = f32[2048,256]{1,0:T(8,128)} reduce(f32[8,2048,256]{2,1,0:T(8,128)} %bitcast.58, f32[]{:T(128)} %constant.85.clone.1), dimensions={0}, to_apply=%region_3.4 | reduce | flops 3670016 | bytes 18874372 | tf_op jit(solution)/shard_map/reduce_sum | solution.py:44
  295.5 6.0 %fusion.20 = f32[512,256]{1,0:T(8,128)S(1)} fusion(f32[2048,512]{0,1:T(8,128)} %bitcast.59, f32[2048,256]{1,0:T(8,128)} %reduce_sum.28), kind=kOutput, calls=%fused_computation.41 | convolution fusion | flops 3221225472 | bytes 6815744 | tf_op jit(solution)/shard_map/dot_general | solution.py:61
  301.5 1.3 collective-permute-start
  303.0 0.7 collective-permute-done
  304.2 50.2 %all-gather.4.cloned.1.call-done = bf16[256,8192]{1,0:T(8,128)(2,1)} async-done(((bf16[8,8192]{1,0:T(8,128)(2,1)}), bf16[256,8192]{1,0:T(8,128)(2,1)}) %all-gather.4.cloned.1.call-update) | async-done | bytes 4194320 | tf_op jit(solution)/shard_map/all_gather | solution.py:81
  354.4 3.4 fusion.1
  357.7 39.5 %all-reduce = (f32[16,256]{1,0:T(8,128)S(1)}, f32[16]{0:T(128)S(1)}) all-reduce(f32[16,256]{1,0:T(8,128)S(1)} %fusion.1, f32[16]{0:T(128)S(1)} %multiply_reduce_fusion), channel_id=1, replica_groups=mesh['dp'=32,'factor'=8] {'factor'}, use_global_device_ids=true, to_apply=%region_4.5 | all-reduce | flops 4112 | bytes 32896 | tf_op jit(solution)/shard_map/psum | solution.py:105
  397.3 1.6 fusion
  398.9 116.2 %reduce-scatter.5.cloned.1.call-done = f32[32,256]{1,0:T(8,128)} async-done(((f32[1024,256]{1,0:T(8,128)}), f32[32,256]{1,0:T(8,128)}) %reduce-scatter.5.cloned.1.call-update) | async-done | bytes 32784 | tf_op jit(solution)/shard_map/reduce_scatter | solution.py:108
  (49 shorter events, 1.9 us)
Async XLA Ops:
  6.5 1.6 copy-start
  6.5 3.3 copy-start.2
  6.5 92.4 %reduce-scatter.7.cloned.1.call-start = ((), (), s32[]{:S(2)}) async-start(), calls=%async_computation.5 | async-start | bytes 2359296
  15.1 1.2 copy-start.8
  15.2 6.4 %copy-start.1 = (bf16[256,256]{1,0:T(8,128)(2,1)S(1)}, bf16[256,256]{1,0:T(8,128)(2,1)}, u32[]{:S(2)}) copy-start(bf16[256,256]{1,0:T(8,128)(2,1)} %param.20) | copy-start | bytes 393220
  15.2 271.8 %all-gather.6.cloned.1.call-start = ((), (), s32[]{:S(2)}) async-start(), calls=%async_computation.4 | async-start | bytes 18874368 | tf_op jit(solution)/shard_map/all_gather | solution.py:44
  24.1 0.8 copy-start.4
  24.1 0.8 copy-start.9
  24.1 1.0 copy-start.3
  24.1 2.6 copy-start.6
  24.1 3.8 copy-start.7
  24.1 4.7 copy-start.5
  24.1 330.2 %all-gather.4.cloned.1.call-start = ((), (), s32[]{:S(2)}) async-start(), calls=%async_computation.2 | async-start | bytes 4325376 | tf_op jit(solution)/shard_map/all_gather | solution.py:81
  26.6 488.5 %reduce-scatter.5.cloned.1.call-start = ((), (), s32[]{:S(2)}) async-start(), calls=%async_computation.3 | async-start | bytes 1081344 | tf_op jit(solution)/shard_map/reduce_scatter | solution.py:108
  301.5 2.1 collective-permute-start
Sparse Core Ops, SparseCore 0:
  15.3 83.6 reduce-scatter.6
  101.6 185.3 all-gather.5
  288.8 65.4 all-gather.3
  399.0 116.0 reduce-scatter.4
